TPU v7x, 512 devices: a whole 4x8x8 slice. The times are simulated.
512 devices in a mesh: segment: 16 (over z, core), mp: 32 (over y, x).
Axes of the slice: x: 4, y: 8, z: 8, core: 2. Of those that a mesh axis runs over, the one named last changes fastest.
Arguments:
- rows: bfloat16 [16, 2, 128, 8192], P('segment', None, None, 'mp'), may hold values from -6 to 6
- carry: bfloat16 [16, 128, 8192], P('segment', None, 'mp'), may hold values from -6 to 6
- weights: bfloat16 [16, 2, 8192, 4096], P('segment', None, None, 'mp'), may hold values from -1.1932427 to 1.1932427
- neighbours: int32 [16, 2, 2, 2], P('segment'), may hold values from 0 to 7, all different within a row
Outputs:
- passed: bfloat16 [16, 128, 8192], P('segment', None, 'mp')
- returned: bfloat16 [16, 128, 8192], P('segment', None, 'mp')
- kv_grad: bfloat16 [1024, 2, 4096], P(None, None, 'mp')
Inputs may be any that keep to these rules, and one draw needn't show every extreme that they name: Each group's 2 neighbours are different pool blocks; pool blocks are numbered by encoder segment in order, then by row.
All inputs are finite; a program needn't handle non-finite values.
Results may differ from a plain program's by a relative error of at most 0.02.
The roundings to bfloat16 on the way count: a program that leaves them out, or rounds other values in their place, can miss the bound.
Values may be sent and summed in bfloat16 or wider, within the bound.
No kernel may reach another device: no remote copies, remote signals or barrier semaphores. Data moves between devices by JAX's collectives and lax.ppermute only.
A program may use at most 64 MiB of HBM per device.

v0:
```python
import math
import jax
import jax.numpy as jnp
from jax import lax
from jax.sharding import PartitionSpec as P

GROUP = 64
NBLEN = 128
NEIGH = 2


def from_behind(x, axis, by):
    devices = lax.axis_size(axis)
    return lax.ppermute(x, axis, [(i, (i + by) % devices) for i in range(devices)])


def attend(queries, key_rows, score_scale):
    scores = (
        jnp.einsum("cqd,ckd->cqk", queries, key_rows, preferred_element_type=jnp.float32)
        * score_scale
    )
    soft = jax.nn.softmax(scores, axis=-1)
    return (soft, soft.astype(jnp.bfloat16))


def attend_back(queries, key_rows, value_rows, soft, rounded, upstream, score_scale):
    d_soft = jnp.einsum("cqd,ckd->cqk", upstream, value_rows, preferred_element_type=jnp.float32)
    grad_values = jnp.einsum("cqk,cqd->ckd", rounded, upstream, preferred_element_type=jnp.float32)
    d_scores = soft * (d_soft - jnp.sum(d_soft * soft, axis=-1, keepdims=True))
    grad_queries = (
        jnp.einsum("cqk,ckd->cqd", d_scores, key_rows.astype(jnp.float32)) * score_scale
    ).astype(jnp.bfloat16)
    grad_keys = jnp.einsum("cqk,cqd->ckd", d_scores, queries.astype(jnp.float32)) * score_scale
    return (grad_queries, grad_keys, grad_values)


def per_device(rows, carry, weights, neighbours):
    segments = lax.axis_size("segment")
    encoders = segments // 4
    first_encoder = segments - encoders
    is_encoder = lax.axis_index("segment") >= first_encoder
    local_rows = rows[0]
    local_carry = carry[0]
    full_rows, full_carry = (
        lax.all_gather(local_rows, "mp", axis=2, tiled=True),
        lax.all_gather(local_carry, "mp", axis=1, tiled=True),
    )
    tokens = local_rows.shape[1]
    width = full_rows.shape[2]
    head = weights.shape[3]
    w_query = weights[0, 0]
    w_out = weights[0, 1]

    def encode():
        flat = full_rows.reshape(2 * tokens, width)
        keyval = jnp.concatenate(
            [
                jnp.dot(flat, w_query, preferred_element_type=jnp.float32),
                jnp.dot(flat, w_out, preferred_element_type=jnp.float32),
            ],
            axis=-1,
        ).astype(jnp.bfloat16)
        return (keyval, jnp.zeros((2 * tokens, head), jnp.bfloat16))

    def decode():
        queries = jnp.dot(
            full_rows.reshape(2 * tokens, width), w_query, preferred_element_type=jnp.float32
        ).astype(jnp.bfloat16)
        return (jnp.zeros((2 * tokens, 2 * head), jnp.bfloat16), queries)

    encoded, queries = lax.cond(is_encoder, encode, decode)
    per_encoder = 2 * tokens // NBLEN
    pool_blocks = encoders * per_encoder
    collected = lax.all_gather(encoded, "segment", axis=0, tiled=True)
    pool = collected[first_encoder * 2 * tokens :].reshape(pool_blocks, NBLEN, 2 * head)
    groups = tokens // GROUP
    local_nbr = neighbours[0]
    score_scale = 1.0 / math.sqrt(head)
    query_blocks = queries.reshape(2, groups, GROUP, head)

    def fetch(batch):
        picked = pool[local_nbr[batch]].reshape(groups, NEIGH * NBLEN, 2 * head)
        return (picked[..., :head], picked[..., head:])

    keys_fwd, values_fwd = fetch(0)
    soft_fwd, rounded_fwd = attend(query_blocks[0], keys_fwd, score_scale)
    mixed = jnp.einsum(
        "cqk,ckd->cqd", rounded_fwd, values_fwd, preferred_element_type=jnp.float32
    ).astype(jnp.bfloat16)
    mixed_flat = mixed.reshape(tokens, head)
    piece = w_out
    out_sum = (
        lax.psum_scatter(
            lax.dot_general(
                piece, mixed_flat, (((1,), (1,)), ((), ())), preferred_element_type=jnp.float32
            ).astype(jnp.bfloat16),
            "mp",
            scatter_dimension=0,
            tiled=True,
        )
        .astype(jnp.float32)
        .T
    )
    forward_rows = (local_rows[0].astype(jnp.float32) + out_sum).astype(jnp.bfloat16)
    forward_rows = jnp.where(is_encoder, local_carry, forward_rows)
    passed = from_behind(forward_rows[None], "segment", 1)
    upstream = (
        jnp.dot(full_carry, w_out, preferred_element_type=jnp.float32)
        .astype(jnp.bfloat16)
        .reshape(groups, GROUP, head)
    )
    keys_back, values_back = fetch(1)
    soft_back, rounded_back = attend(query_blocks[1], keys_back, score_scale)
    grad_queries, grad_keys, grad_values = attend_back(
        query_blocks[1], keys_back, values_back, soft_back, rounded_back, upstream, score_scale
    )
    grad_flat = grad_queries.reshape(tokens, head)
    piece = w_query
    grad_input = (
        lax.psum_scatter(
            lax.dot_general(
                piece, grad_flat, (((1,), (1,)), ((), ())), preferred_element_type=jnp.float32
            ).astype(jnp.bfloat16),
            "mp",
            scatter_dimension=0,
            tiled=True,
        )
        .astype(jnp.float32)
        .T
    )
    back = local_carry.astype(jnp.float32) + grad_input
    back_rows = jnp.where(is_encoder, local_carry, back.astype(jnp.bfloat16))
    returned = from_behind(back_rows[None], "segment", -1)
    onehot = (
        local_nbr[1][..., None] == jnp.arange(pool_blocks, dtype=jnp.int32)[None, None, :]
    ).astype(jnp.float32)
    grad_keyval = jnp.concatenate([grad_keys, grad_values], axis=-1).reshape(
        groups, NEIGH, NBLEN, 2 * head
    )
    contrib = jnp.einsum("cbp,cbrf->prf", onehot, grad_keyval)
    contrib = jnp.where(is_encoder, jnp.zeros_like(contrib), contrib)
    pooled = lax.psum(contrib.astype(jnp.bfloat16), "segment").astype(jnp.float32)
    kv_grad = pooled.reshape(pool_blocks * NBLEN, 2, head).astype(jnp.bfloat16)
    return (passed, returned, kv_grad)


def solution(mesh):
    placed = (
        P("segment", None, None, "mp"),
        P("segment", None, "mp"),
        P("segment", None, None, "mp"),
        P("segment", None, None, None),
    )
    return jax.shard_map(
        per_device,
        mesh=mesh,
        in_specs=placed,
        out_specs=(P("segment", None, "mp"), P("segment", None, "mp"), P(None, None, "mp")),
        check_vma=False,
    )
```

profile of v0, /device:TPU:1, one launch (start us, length us, event | category | flops | bytes accessed | tf_op | source)
XLA Modules:
  0.0 812.3 jit_solution(813906581693303927)
XLA Ops:
  7.2 0.7 all-gather.8.cloned.1.call-update
  7.9 0.7 all-gather.10.cloned.1.call-update
  8.7 3.8 slice_bitcast_fusion
  12.5 89.2 %all-gather.8.cloned.1.call-done = bf16[1,2,128,8192]{3,2,1,0:T(8,128)(2,1)} async-done(((bf16[1,2,128,256]{3,2,1,0:T(8,128)(2,1)}), bf16[1,2,128,8192]{3,2,1,0:T(8,128)(2,1)}) %all-gather.8.cloned.1.call-update) | async-done | bytes 4194320 | tf_op jit(solution)/shard_map/all_gather | solution.py:45
  101.8 3.5 conditional.1
  101.8 3.4 convolution_convert_fusion
  105.3 0.6 copy-done.1
  106.1 79.5 %all-gather.10.cloned.1.call-done = bf16[1,128,8192]{2,1,0:T(8,128)(2,1)} async-done(((bf16[1,128,256]{2,1,0:T(8,128)(2,1)}), bf16[1,128,8192]{2,1,0:T(8,128)(2,1)}) %all-gather.10.cloned.1.call-update) | async-done | bytes 2097168 | tf_op jit(solution)/shard_map/all_gather | solution.py:46
  185.7 2.9 fusion.13
  188.6 45.9 %all-gather.6.cloned.1.call-done = bf16[4096,256]{1,0:T(8,128)(2,1)} async-done(((bf16[256,256]{1,0:T(8,128)(2,1)}), bf16[4096,256]{1,0:T(8,128)(2,1)}) %all-gather.6.cloned.1.call-update) | async-done | bytes 2097168 | tf_op jit(solution)/shard_map/all_gather | solution.py:74
  234.5 1.1 slice.67
  235.6 0.6 gather_fusion.1
  236.3 0.4 fusion.37
  236.9 0.3 fusion.12
  237.3 3.7 fusion.3
  241.1 0.6 gather_fusion
  242.0 0.3 convolution_convert_fusion.5
  242.4 3.6 fusion.2
  246.1 0.3 fusion.28
  246.5 0.4 convolution_multiply_fusion
  247.0 0.5 copy.12
  247.5 0.5 fusion.7
  248.0 0.6 copy.13
  248.6 1.0 convert_element_type.80
  249.6 205.3 %reduce-scatter.5.cloned.1.call-done = bf16[256,128]{0,1:T(8,128)(2,1)} async-done(((bf16[8192,128]{0,1:T(8,128)(2,1)}), bf16[256,128]{0,1:T(8,128)(2,1)}) %reduce-scatter.5.cloned.1.call-update) | async-done | bytes 65552 | tf_op jit(solution)/shard_map/reduce_scatter | solution.py:120
  454.9 224.9 %reduce-scatter.3.cloned.1.call-done = bf16[256,128]{0,1:T(8,128)(2,1)} async-done(((bf16[8192,128]{0,1:T(8,128)(2,1)}), bf16[256,128]{0,1:T(8,128)(2,1)}) %reduce-scatter.3.cloned.1.call-update) | async-done | bytes 65552 | tf_op jit(solution)/shard_map/reduce_scatter | solution.py:93
  679.8 0.9 fusion.25
  680.7 6.9 collective-permute-start
  687.6 114.5 %all-reduce.2.cloned.1.call-done = bf16[1024,2,128]{0,2,1:T(8,128)(2,1)} async-done(((bf16[1024,2,128]{0,2,1:T(8,128)(2,1)}), bf16[1024,2,128]{0,2,1:T(8,128)(2,1)}) %all-reduce.2.cloned.1.call-update) | async-done | bytes 524304 | tf_op jit(solution)/shard_map/psum | solution.py:142
  802.1 2.0 copy.14
  804.1 0.6 copy.25
  804.8 0.6 copy.26
  (35 shorter events, 1.5 us)
Async XLA Ops:
  7.2 94.6 %all-gather.8.cloned.1.call-start = ((), (), s32[]{:S(2)}) async-start(), calls=%async_computation.6 | async-start | bytes 4325376 | tf_op jit(solution)/shard_map/all_gather | solution.py:45
  7.9 177.8 %all-gather.10.cloned.1.call-start = ((), (), s32[]{:S(2)}) async-start(), calls=%async_computation.7 | async-start | bytes 2162688 | tf_op jit(solution)/shard_map/all_gather | solution.py:46
  8.6 225.9 %all-gather.6.cloned.1.call-start = ((), (), s32[]{:S(2)}) async-start(), calls=%async_computation.2 | async-start | bytes 2228224 | tf_op jit(solution)/shard_map/all_gather | solution.py:74
  101.8 4.2 copy-start.4
  105.3 0.7 copy-start.1
  106.0 348.9 %reduce-scatter.5.cloned.1.call-start = ((), (), s32[]{:S(2)}) async-start(), calls=%async_computation.4 | async-start | bytes 2162688 | tf_op jit(solution)/shard_map/reduce_scatter | solution.py:120
  241.0 438.8 %reduce-scatter.3.cloned.1.call-start = ((), (), s32[]{:S(2)}) async-start(), calls=%async_computation.3 | async-start | bytes 2162688 | tf_op jit(solution)/shard_map/reduce_scatter | solution.py:93
  246.0 556.2 %all-reduce.2.cloned.1.call-start = ((), (), s32[]{:S(2)}) async-start(), calls=%async_computation.5 | async-start | bytes 1048576 | tf_op jit(solution)/shard_map/psum | solution.py:142
  247.5 432.3 %copy-start.2 = (bf16[1,2,128,256]{3,2,1,0:T(8,128)(2,1)S(1)}, bf16[1,2,128,256]{3,2,1,0:T(8,128)(2,1)}, u32[]{:S(2)}) copy-start(bf16[1,2,128,256]{3,2,1,0:T(8,128)(2,1)} %param.6) | copy-start | bytes 393220
  247.5 432.3 %copy-start.3 = (bf16[1,128,256]{2,1,0:T(8,128)(2,1)S(1)}, bf16[1,128,256]{2,1,0:T(8,128)(2,1)}, u32[]{:S(2)}) copy-start(bf16[1,128,256]{2,1,0:T(8,128)(2,1)} %param.7) | copy-start | bytes 196612
  680.7 123.5 %collective-permute-start = (bf16[1,128,256]{2,1,0:T(8,128)(2,1)S(1)}, bf16[1,128,256]{2,1,0:T(8,128)(2,1)S(1)}, u32[]{:S(2)}, u32[]{:S(2)}) collective-permute-start(bf16[1,128,256]{2,1,0:T(8,128)(2,1)S(1)} %get-tuple-element.53), channel_id=1, source_target_pairs={{0,32},{32,64},{64,96},{96,128},{128,160},{160,192},{192,224},{224... | collective-permute-start | bytes 196616 | tf_op jit(solution)/shard_map/ppermute | solution.py:14
  687.6 116.5 %collective-permute-start.1 = (bf16[1,128,256]{2,1,0:T(8,128)(2,1)S(1)}, bf16[1,128,256]{2,1,0:T(8,128)(2,1)S(1)}, u32[]{:S(2)}, u32[]{:S(2)}) collective-permute-start(bf16[1,128,256]{2,1,0:T(8,128)(2,1)S(1)} %get-tuple-element.52), channel_id=1, source_target_pairs={{0,480},{32,0},{64,32},{96,64},{128,96},{160,128},{192,160},{224,1... | collective-permute-start | bytes 196616 | tf_op jit(solution)/shard_map/ppermute | solution.py:14
Sparse Core Ops, SparseCore 0:
  11.0 90.6 all-gather.7
  104.8 80.7 all-gather.9
  188.4 46.0 all-gather.5
  241.1 213.7 reduce-scatter.4
  459.8 219.9 reduce-scatter.2
  682.5 119.5 all-reduce.1
where the time goes:
time: 813 us; the launch traced here: 812 us
  waiting for transfers between devices  761 us (94%)
  matrix products  16.1 us (2%)
  between operations  14.3 us (2%)
  local copies, waits for them, and re-layouts  12.4 us (2%)
    reduce_scatter x1, waiting for transfers between devices, per_device(): lax.psum_scatter(lax.dot_general(piece, mixed_flat, (((1,), (1,)), ((), (...  225 us
    reduce_scatter x1, waiting for transfers between devices, per_device(): lax.psum_scatter(lax.dot_general(piece, grad_flat, (((1,), (1,)), ((), ()...  205 us
    psum x1, waiting for transfers between devices, per_device(): lax.psum(contrib.astype(jnp.bfloat16), 'segment').astype(jnp.float32)  115 us
    all_gather x1, waiting for transfers between devices, per_device(): lax.all_gather(local_rows, 'mp', axis=2, tiled=True)  89.2 us
    all_gather x1, waiting for transfers between devices, per_device(): lax.all_gather(local_carry, 'mp', axis=1, tiled=True)  79.5 us
    all_gather x1, waiting for transfers between devices, per_device(): collected = lax.all_gather(encoded, 'segment', axis=0, tiled=True)  45.9 us
  transfers between devices with their start and end apart: 8, of which 6 were waited for; matrix products, arithmetic and copies ran while one was open for 3% of the time, Pallas kernels for 0%

commit v1 on v0

--- a/solution.py
+++ b/solution.py
@@ -7,6 +7,12 @@
 GROUP = 64
 NBLEN = 128
 NEIGH = 2
+
+
+def gather_from_all(x, axis, dim):
+    size = lax.axis_size(axis)
+    repeats = [size if d == dim else 1 for d in range(x.ndim)]
+    return lax.all_to_all(jnp.tile(x, repeats), axis, split_axis=dim, concat_axis=dim, tiled=True)
 
 
 def from_behind(x, axis, by):
@@ -43,7 +49,7 @@
     local_carry = carry[0]
     full_rows, full_carry = (
         lax.all_gather(local_rows, "mp", axis=2, tiled=True),
-        lax.all_gather(local_carry, "mp", axis=1, tiled=True),
+        gather_from_all(local_carry, "mp", 1),
     )
     tokens = local_rows.shape[1]
     width = full_rows.shape[2]

time: 813 us -> 752 us (0.925)
  waiting for transfers between devices: 761 us -> 684 us
  starting transfers between devices: 7.19 us -> 17.8 us
    all_gather x1 -> x0, waiting for transfers between devices: 79.5 us -> none  [per_device(): lax.all_gather(local_carry, 'mp', axis=1, tiled=True)]
    all_to_all x0 -> x1, starting transfers between devices: none -> 10.6 us  [gather_from_all(): lax.all_to_all(jnp.tile(x, repeats), axis, split_axis=dim, concat_axis=di...]
  transfers between devices with their start and end apart: 8 -> 8, of which waited for: 6 -> 5; matrix products, arithmetic and copies ran while one was open for 3% -> 4% of each run, Pallas kernels for 0% -> 0%
where the time goes in v1:
time: 752 us; the launch traced here: 751 us
  waiting for transfers between devices  684 us (91%)
  local copies, waits for them, and re-layouts  18.1 us (2%)
  starting transfers between devices  17.8 us (2%)
  matrix products  15.5 us (2%)
  between operations  13.9 us (2%)
    reduce_scatter x1, waiting for transfers between devices, per_device(): lax.psum_scatter(lax.dot_general(piece, mixed_flat, (((1,), (1,)), ((), (...  225 us
    reduce_scatter x1, waiting for transfers between devices, per_device(): lax.psum_scatter(lax.dot_general(piece, grad_flat, (((1,), (1,)), ((), ()...  205 us
    psum x1, waiting for transfers between devices, per_device(): lax.psum(contrib.astype(jnp.bfloat16), 'segment').astype(jnp.float32)  115 us
    all_gather x1, waiting for transfers between devices, per_device(): lax.all_gather(local_rows, 'mp', axis=2, tiled=True)  95.9 us
    all_gather x1, waiting for transfers between devices, per_device(): collected = lax.all_gather(encoded, 'segment', axis=0, tiled=True)  43 us
  transfers between devices with their start and end apart: 8, of which 5 were waited for; matrix products, arithmetic and copies ran while one was open for 4% of the time, Pallas kernels for 0%

profile of v1, /device:TPU:1, one launch (start us, length us, event | category | flops | bytes accessed | tf_op | source)
XLA Modules:
  0.0 751.1 jit_solution(16535631230419899332)
XLA Ops:
  7.2 0.7 all-gather.6.cloned.1.call-update
  7.9 2.4 tile.2
  10.3 10.6 %all-to-all-start = ((bf16[128,32,256]{2,0,1:T(8,128)(2,1)}), bf16[128,32,256]{2,0,1:T(8,128)(2,1)}, u32[]{:S(2)}, u32[]{:S(2)}) async-start(bf16[128,32,256]{2,0,1:T(8,128)(2,1)} %tile.2), calls=%async_computation.1 | async-start | bytes 4194304 | tf_op jit(solution)/shard_map/all_to_all | solution.py:15
  21.0 3.9 slice_bitcast_fusion
  24.9 95.9 %all-gather.6.cloned.1.call-done = bf16[1,2,128,8192]{3,2,1,0:T(8,128)(2,1)} async-done(((bf16[1,2,128,256]{3,2,1,0:T(8,128)(2,1)}), bf16[1,2,128,8192]{3,2,1,0:T(8,128)(2,1)}) %all-gather.6.cloned.1.call-update) | async-done | bytes 4194320 | tf_op jit(solution)/shard_map/all_gather | solution.py:51
  120.8 3.5 conditional.1
  120.8 3.4 convolution_convert_fusion
  124.3 0.6 copy-done.1
  125.1 3.2 copy.21
  128.4 2.3 convolution_convert_fusion.5
  130.7 43.0 %all-gather.4.cloned.1.call-done = bf16[4096,256]{1,0:T(8,128)(2,1)} async-done(((bf16[256,256]{1,0:T(8,128)(2,1)}), bf16[4096,256]{1,0:T(8,128)(2,1)}) %all-gather.4.cloned.1.call-update) | async-done | bytes 2097168 | tf_op jit(solution)/shard_map/all_gather | solution.py:80
  173.7 1.1 slice.67
  174.8 0.6 gather_fusion.1
  175.5 0.4 fusion.32
  176.2 0.3 fusion.10
  176.5 3.7 fusion.3
  180.3 0.6 gather_fusion
  181.6 3.6 fusion.2
  185.3 0.3 fusion.23
  185.7 0.4 convolution_multiply_fusion
  186.2 0.5 copy.23
  186.7 0.5 fusion.5
  187.2 0.6 copy.24
  187.8 1.0 convert_element_type.80
  188.8 205.2 %reduce-scatter.5.cloned.1.call-done = bf16[256,128]{0,1:T(8,128)(2,1)} async-done(((bf16[8192,128]{0,1:T(8,128)(2,1)}), bf16[256,128]{0,1:T(8,128)(2,1)}) %reduce-scatter.5.cloned.1.call-update) | async-done | bytes 65552 | tf_op jit(solution)/shard_map/reduce_scatter | solution.py:126
  394.1 224.9 %reduce-scatter.3.cloned.1.call-done = bf16[256,128]{0,1:T(8,128)(2,1)} async-done(((bf16[8192,128]{0,1:T(8,128)(2,1)}), bf16[256,128]{0,1:T(8,128)(2,1)}) %reduce-scatter.3.cloned.1.call-update) | async-done | bytes 65552 | tf_op jit(solution)/shard_map/reduce_scatter | solution.py:99
  619.0 0.9 fusion.20
  619.9 6.9 collective-permute-start
  626.8 114.5 %all-reduce.2.cloned.1.call-done = bf16[1024,2,128]{0,2,1:T(8,128)(2,1)} async-done(((bf16[1024,2,128]{0,2,1:T(8,128)(2,1)}), bf16[1024,2,128]{0,2,1:T(8,128)(2,1)}) %all-reduce.2.cloned.1.call-update) | async-done | bytes 524304 | tf_op jit(solution)/shard_map/psum | solution.py:148
  741.3 2.0 copy.25
  743.3 0.6 copy.36
  744.0 0.6 copy.37
  (36 shorter events, 1.8 us)
Async XLA Ops:
  7.2 113.6 %all-gather.6.cloned.1.call-start = ((), (), s32[]{:S(2)}) async-start(), calls=%async_computation.7 | async-start | bytes 4325376 | tf_op jit(solution)/shard_map/all_gather | solution.py:51
  10.3 114.8 %all-to-all-start = ((bf16[128,32,256]{2,0,1:T(8,128)(2,1)}), bf16[128,32,256]{2,0,1:T(8,128)(2,1)}, u32[]{:S(2)}, u32[]{:S(2)}) async-start(bf16[128,32,256]{2,0,1:T(8,128)(2,1)} %tile.2), calls=%async_computation.1 | async-start | bytes 4194304 | tf_op jit(solution)/shard_map/all_to_all | solution.py:15
  21.0 152.7 %all-gather.4.cloned.1.call-start = ((), (), s32[]{:S(2)}) async-start(), calls=%async_computation.3 | async-start | bytes 2228224 | tf_op jit(solution)/shard_map/all_gather | solution.py:80
  120.8 4.2 copy-start.4
  124.3 0.7 copy-start.1
  125.0 269.1 %reduce-scatter.5.cloned.1.call-start = ((), (), s32[]{:S(2)}) async-start(), calls=%async_computation.5 | async-start | bytes 2162688 | tf_op jit(solution)/shard_map/reduce_scatter | solution.py:126
  180.2 438.8 %reduce-scatter.3.cloned.1.call-start = ((), (), s32[]{:S(2)}) async-start(), calls=%async_computation.4 | async-start | bytes 2162688 | tf_op jit(solution)/shard_map/reduce_scatter | solution.py:99
  185.2 556.1 %all-reduce.2.cloned.1.call-start = ((), (), s32[]{:S(2)}) async-start(), calls=%async_computation.6 | async-start | bytes 1048576 | tf_op jit(solution)/shard_map/psum | solution.py:148
  186.7 432.3 %copy-start.2 = (bf16[1,2,128,256]{3,2,1,0:T(8,128)(2,1)S(1)}, bf16[1,2,128,256]{3,2,1,0:T(8,128)(2,1)}, u32[]{:S(2)}) copy-start(bf16[1,2,128,256]{3,2,1,0:T(8,128)(2,1)} %param.6) | copy-start | bytes 393220
  186.7 432.3 %copy-start.3 = (bf16[1,128,256]{2,1,0:T(8,128)(2,1)S(1)}, bf16[1,128,256]{2,1,0:T(8,128)(2,1)}, u32[]{:S(2)}) copy-start(bf16[1,128,256]{2,1,0:T(8,128)(2,1)} %param.7) | copy-start | bytes 196612
  619.9 123.4 %collective-permute-start = (bf16[1,128,256]{2,1,0:T(8,128)(2,1)S(1)}, bf16[1,128,256]{2,1,0:T(8,128)(2,1)S(1)}, u32[]{:S(2)}, u32[]{:S(2)}) collective-permute-start(bf16[1,128,256]{2,1,0:T(8,128)(2,1)S(1)} %get-tuple-element.65), channel_id=1, source_target_pairs={{0,32},{32,64},{64,96},{96,128},{128,160},{160,192},{192,224},{224... | collective-permute-start | bytes 196616 | tf_op jit(solution)/shard_map/ppermute | solution.py:20
  626.8 116.5 %collective-permute-start.1 = (bf16[1,128,256]{2,1,0:T(8,128)(2,1)S(1)}, bf16[1,128,256]{2,1,0:T(8,128)(2,1)S(1)}, u32[]{:S(2)}, u32[]{:S(2)}) collective-permute-start(bf16[1,128,256]{2,1,0:T(8,128)(2,1)S(1)} %get-tuple-element.64), channel_id=1, source_target_pairs={{0,480},{32,0},{64,32},{96,64},{128,96},{160,128},{192,160},{224,1... | collective-permute-start | bytes 196616 | tf_op jit(solution)/shard_map/ppermute | solution.py:20
Sparse Core Ops, SparseCore 0:
  11.0 109.7 all-gather.5
  125.1 48.5 all-gather.3
  180.3 213.7 reduce-scatter.4
  399.0 219.9 reduce-scatter.2
  621.7 119.5 all-reduce.1
